TPU v7x, 32 devices: a whole 2x2x4 slice. The times are simulated.
32 devices in a mesh: groups: 2 (over y), tensor: 4 (over x, core), dp: 4 (over z).
Axes of the slice: x: 2, y: 2, z: 4, core: 2. Of those that a mesh axis runs over, the one named last changes fastest.
Arguments:
- tokens: bfloat16 [65536, 4096], P(('groups', 'dp'), 'tensor'), parts along dimension 0, may hold values from -6 to 6
- cotangent: bfloat16 [65536, 4096], P(('groups', 'dp'), 'tensor'), parts along dimension 0, may hold values from -6 to 6
- w_first: bfloat16 [16, 256, 256], P('tensor'), may hold values from -0.375 to 0.375
- w_second: bfloat16 [16, 256, 256], P('tensor'), may hold values from -0.375 to 0.375
Outputs:
- grad_tokens: bfloat16 [65536, 4096], P(('groups', 'dp'), 'tensor'), parts along dimension 0
- grad_first: float32 [32, 256, 256], P(('groups', 'tensor'), 'dp'), parts along dimension 0
- grad_second: float32 [32, 256, 256], P(('groups', 'tensor'), 'dp'), parts along dimension 0
There are 2 independent parts, one for each index of `groups`. A program takes and returns all parts, laid end to end along the dimension named above; an argument that names none is the same for every part. Nothing has to cross between parts.
All inputs are finite; a program needn't handle non-finite values.
Results may differ from a plain program's by a relative error of at most 0.0065.
Values may be sent and summed in bfloat16 or wider, within the bound.
No kernel may reach another device: no remote copies, remote signals or barrier semaphores. Data moves between devices by JAX's collectives and lax.ppermute only.
A program may use at most 192 MiB of HBM per device.

v0:
```python
import math
import jax
import jax.numpy as jnp
from jax import lax
from jax.sharding import PartitionSpec as P

NB = 16
CHUNKS = 4


def expanded_weights(w_first, w_second, n_dev):
    blk_local, bs, _ = w_first.shape
    sub = bs // NB
    eye = jnp.eye(blk_local, dtype=jnp.bool_)
    zero = jnp.zeros((), w_first.dtype)
    w1r = w_first.reshape(blk_local, bs, n_dev, blk_local, sub)
    w1p = jnp.where(eye[:, None, None, None, :, None], w1r[:, :, :, :, None, :], zero).reshape(
        blk_local * bs, blk_local * bs
    )
    w2r = w_second.reshape(blk_local, sub, n_dev, blk_local, bs).transpose(0, 4, 2, 3, 1)
    w2p = jnp.where(eye[:, None, None, :, None, None], w2r[:, :, :, None, :, :], zero).reshape(
        blk_local * bs, blk_local * bs
    )
    w1t = w_first.reshape(blk_local, bs, NB, sub).transpose(2, 3, 0, 1)
    w1tp = jnp.where(eye[None, :, None, :, None], w1t[:, None, :, :, :], zero).reshape(
        blk_local * bs, blk_local * bs
    )
    return (w1p, w2p, w1tp)


def shards(tokens, cotangent, w_first, w_second):
    tok_rows = tokens.shape[0]
    blk_local, bs, _ = w_first.shape
    feat = blk_local * bs
    sub = bs // NB
    n_dev = lax.axis_size("tensor")
    dp_count = lax.axis_size("dp")
    grad_scale = 1.0 / math.sqrt(tok_rows * dp_count)
    w1p, w2p, w1tp = expanded_weights(w_first, w_second, n_dev)
    step = tok_rows // CHUNKS
    gf_acc = None
    gs_acc = None
    outs = []
    for k in range(CHUNKS):
        x = tokens[k * step : (k + 1) * step]
        cot = cotangent[k * step : (k + 1) * step]
        hidden = jnp.dot(x, w1p, preferred_element_type=jnp.float32).astype(jnp.bfloat16)
        moved = lax.all_to_all(
            hidden.reshape(step, n_dev, feat // n_dev), "tensor", 1, 1, tiled=True
        ).reshape(step, feat)
        active = jnp.maximum(moved, jnp.zeros((), jnp.bfloat16))
        gs = lax.dot_general(
            active, cot, (((0,), (0,)), ((), ())), preferred_element_type=jnp.float32
        )
        backed = jnp.dot(cot, w2p, preferred_element_type=jnp.float32)
        masked = jnp.where(moved > 0, backed, 0.0).astype(jnp.bfloat16)
        returned = lax.all_to_all(
            masked.reshape(step, n_dev, feat // n_dev), "tensor", 1, 1, tiled=True
        ).reshape(step, feat)
        gt = jnp.dot(returned, w1tp, preferred_element_type=jnp.float32).astype(jnp.bfloat16)
        outs.append(gt)
        gf = lax.dot_general(
            x, returned, (((0,), (0,)), ((), ())), preferred_element_type=jnp.float32
        )
        gf_acc = gf if gf_acc is None else gf_acc + gf
        gs_acc = gs if gs_acc is None else gs_acc + gs
    grad_tokens = jnp.concatenate(outs, axis=0)
    gf5 = gf_acc.reshape(blk_local, bs, NB, blk_local, sub)
    first_term = jnp.diagonal(gf5, axis1=0, axis2=3).transpose(3, 0, 1, 2)
    first_term = first_term.reshape(blk_local, bs, bs) * grad_scale
    gs6 = gs_acc.reshape(n_dev, blk_local, blk_local, sub, blk_local, bs)
    gsd = jnp.diagonal(gs6, axis1=1, axis2=4)
    second_term = gsd.transpose(4, 2, 0, 1, 3).reshape(blk_local, bs, bs) * grad_scale
    grad_first, grad_second = (
        lax.psum_scatter(first_term, "dp", scatter_dimension=1, tiled=True),
        lax.psum_scatter(second_term, "dp", scatter_dimension=1, tiled=True),
    )
    return (grad_tokens, grad_first, grad_second)


def solution(mesh):
    return jax.shard_map(
        shards,
        mesh=mesh,
        in_specs=(
            P(("groups", "dp"), "tensor"),
            P(("groups", "dp"), "tensor"),
            P("tensor", None, None),
            P("tensor", None, None),
        ),
        out_specs=(
            P(("groups", "dp"), "tensor"),
            P(("groups", "tensor"), "dp", None),
            P(("groups", "tensor"), "dp", None),
        ),
        check_vma=False,
    )
```

profile of v0, /device:TPU:0, one launch (start us, length us, event | category | flops | bytes accessed | tf_op | source)
XLA Modules:
  0.0 582.0 jit_solution(16535600350372632069)
XLA Ops:
  12.5 9.1 %convolution_convert_fusion.3 = bf16[1024,2048]{1,0:T(8,128)(2,1)} fusion(bf16[1024,1024]{0,1:T(8,128)(2,1)S(1)} %bitcast.136, bf16[8192,1024]{1,0:T(8,128)(2,1)} %param.4), kind=kOutput, calls=%fused_computation.18 | convolution fusion | flops 4297064448 | bytes 10485760 | tf_op jit(solution)/shard_map/dot_general | solution.py:47
  26.5 9.3 %convolution_convert_fusion.5 = bf16[1024,2048]{1,0:T(8,128)(2,1)} fusion(bf16[1024,1024]{0,1:T(8,128)(2,1)} %bitcast.137, bf16[8192,1024]{1,0:T(8,128)(2,1)} %param.4), kind=kOutput, calls=%fused_computation.20 | convolution fusion | flops 4297064448 | bytes 10485760 | tf_op jit(solution)/shard_map/dot_general | solution.py:47
  35.8 39.5 %all-to-all-done.4 = bf16[2048,4,256]{0,2,1:T(8,128)(2,1)} async-done(((bf16[2048,4,256]{0,2,1:T(8,128)(2,1)}), bf16[2048,4,256]{0,2,1:T(8,128)(2,1)}, u32[]{:S(2)}, u32[]{:S(2)}) %all-to-all-start.4) | async-done | bytes 4194336 | tf_op jit(solution)/shard_map/all_to_all | solution.py:48
  75.3 5.3 all-to-all-start.2
  80.7 9.4 %convolution_convert_fusion.7 = bf16[1024,2048]{1,0:T(8,128)(2,1)} fusion(bf16[1024,1024]{0,1:T(8,128)(2,1)} %bitcast.138, bf16[8192,1024]{1,0:T(8,128)(2,1)} %param.4), kind=kOutput, calls=%fused_computation.22 | convolution fusion | flops 4297064448 | bytes 10485760 | tf_op jit(solution)/shard_map/dot_general | solution.py:47
  90.0 38.8 %all-to-all-done.2 = bf16[2048,4,256]{0,2,1:T(8,128)(2,1)} async-done(((bf16[2048,4,256]{0,2,1:T(8,128)(2,1)}), bf16[2048,4,256]{0,2,1:T(8,128)(2,1)}, u32[]{:S(2)}, u32[]{:S(2)}) %all-to-all-start.2) | async-done | bytes 4194336 | tf_op jit(solution)/shard_map/all_to_all | solution.py:48
  140.0 8.3 %convolution_convert_fusion.1 = bf16[1024,2048]{1,0:T(8,128)(2,1)} fusion(bf16[1024,1024]{0,1:T(8,128)(2,1)S(1)} %bitcast.139, bf16[8192,1024]{1,0:T(8,128)(2,1)} %param.4), kind=kOutput, calls=%fused_computation.16 | convolution fusion | flops 4297064448 | bytes 10485760 | tf_op jit(solution)/shard_map/dot_general | solution.py:47
  148.3 33.7 %all-to-all-done = bf16[2048,4,256]{0,2,1:T(8,128)(2,1)} async-done(((bf16[2048,4,256]{0,2,1:T(8,128)(2,1)}), bf16[2048,4,256]{0,2,1:T(8,128)(2,1)}, u32[]{:S(2)}, u32[]{:S(2)}) %all-to-all-start) | async-done | bytes 4194336 | tf_op jit(solution)/shard_map/all_to_all | solution.py:48
  202.7 8.3 %fusion.1 = bf16[2048,1024]{0,1:T(8,128)(2,1)} fusion(pred[2048,4,256]{0,2,1:T(32,128)(4,1)S(1)} %broadcast_compare_fusion.1, bf16[1024,1024]{0,1:T(8,128)(2,1)S(1)} %bitcast.132, bf16[8192,1024]{1,0:T(8,128)(2,1)} %param.5), kind=kOutput, calls=%fused_computation.6 | convolution fusion | flops 4299161600 | bytes 12582912 | tf_op jit(solution)/shard_map/dot_general | solution.py:55
  210.9 24.3 %all-to-all-done.6 = bf16[2048,4,256]{0,2,1:T(8,128)(2,1)} async-done(((bf16[2048,4,256]{0,2,1:T(8,128)(2,1)}), bf16[2048,4,256]{0,2,1:T(8,128)(2,1)}, u32[]{:S(2)}, u32[]{:S(2)}) %all-to-all-start.6) | async-done | bytes 4194336 | tf_op jit(solution)/shard_map/all_to_all | solution.py:48
  249.3 8.5 %fusion.2 = bf16[2048,1024]{0,1:T(8,128)(2,1)} fusion(pred[2048,4,256]{0,2,1:T(32,128)(4,1)S(1)} %broadcast_compare_fusion.2, bf16[1024,1024]{0,1:T(8,128)(2,1)S(1)} %bitcast.133, bf16[8192,1024]{1,0:T(8,128)(2,1)} %param.5), kind=kOutput, calls=%fused_computation.8 | convolution fusion | flops 4299161600 | bytes 12582912 | tf_op jit(solution)/shard_map/dot_general | solution.py:55
  257.8 8.2 %fusion.10 = f32[1024,1024]{1,0:T(8,128)} fusion(bf16[2048,1024]{0,1:T(8,128)(2,1)S(1)} %bitcast.117, bf16[8192,1024]{1,0:T(8,128)(2,1)} %param.5), kind=kOutput, calls=%fused_computation.29 | convolution fusion | flops 4294967296 | bytes 12582912 | tf_op jit(solution)/shard_map/dot_general | solution.py:52
  266.0 22.3 %all-to-all-done.5 = bf16[2048,4,256]{0,2,1:T(8,128)(2,1)} async-done(((bf16[2048,4,256]{0,2,1:T(8,128)(2,1)}), bf16[2048,4,256]{0,2,1:T(8,128)(2,1)}, u32[]{:S(2)}, u32[]{:S(2)}) %all-to-all-start.5) | async-done | bytes 4194336 | tf_op jit(solution)/shard_map/all_to_all | solution.py:57
  298.2 8.4 %fusion = bf16[2048,1024]{0,1:T(8,128)(2,1)} fusion(pred[2048,4,256]{0,2,1:T(32,128)(4,1)S(1)} %copy-done.6, bf16[1024,1024]{0,1:T(8,128)(2,1)S(1)} %bitcast.134, bf16[8192,1024]{1,0:T(8,128)(2,1)} %param.5), kind=kOutput, calls=%fused_computation.4 | convolution fusion | flops 4299161600 | bytes 12582912 | tf_op jit(solution)/shard_map/dot_general | solution.py:55
  306.6 8.3 %fusion.16 = f32[1024,1024]{1,0:T(8,128)} fusion(bf16[2048,1024]{0,1:T(8,128)(2,1)S(1)} %bitcast.115, bf16[8192,1024]{1,0:T(8,128)(2,1)} %param.5), kind=kOutput, calls=%fused_computation.35 | convolution fusion | flops 4294967296 | bytes 12582912 | tf_op jit(solution)/shard_map/dot_general | solution.py:52
  315.0 8.2 %fusion.4 = f32[1024,1024]{1,0:T(8,128)} fusion(bf16[2048,1024]{0,1:T(8,128)(2,1)S(1)} %bitcast.118, bf16[8192,1024]{1,0:T(8,128)(2,1)} %param.5), kind=kOutput, calls=%fused_computation.23 | convolution fusion | flops 4294967296 | bytes 12582912 | tf_op jit(solution)/shard_map/dot_general | solution.py:52
  323.2 18.6 %all-to-all-done.3 = bf16[2048,4,256]{0,2,1:T(8,128)(2,1)} async-done(((bf16[2048,4,256]{0,2,1:T(8,128)(2,1)}), bf16[2048,4,256]{0,2,1:T(8,128)(2,1)}, u32[]{:S(2)}, u32[]{:S(2)}) %all-to-all-start.3) | async-done | bytes 4194336 | tf_op jit(solution)/shard_map/all_to_all | solution.py:57
  346.7 13.7 %add_add_fusion = f32[1024,1024]{1,0:T(8,128)} fusion(f32[1024,1024]{1,0:T(8,128)} %fusion.4, f32[1024,1024]{1,0:T(8,128)} %fusion.10, f32[1024,1024]{1,0:T(8,128)} %fusion.16, bf16[2048,1024]{0,1:T(8,128)(2,1)} %bitcast.123, bf16[8192,1024]{1,0:T(8,128)(2,1)} %param.5), kind=kOutput, calls=%fused_computation.13 | convolution fusion | flops 4298113024 | bytes 25165824 | tf_op jit(solution)/shard_map/dot_general | solution.py:52
  360.3 5.6 reshape.154
  379.0 8.4 %fusion.3 = bf16[2048,1024]{0,1:T(8,128)(2,1)} fusion(pred[2048,4,256]{0,2,1:T(32,128)(4,1)S(1)} %broadcast_compare_fusion.3, bf16[1024,1024]{0,1:T(8,128)(2,1)S(1)} %bitcast.135, bf16[8192,1024]{1,0:T(8,128)(2,1)} %param.5), kind=kOutput, calls=%fused_computation.10 | convolution fusion | flops 4299161600 | bytes 12582912 | tf_op jit(solution)/shard_map/dot_general | solution.py:55
  387.3 10.0 %fusion.13 = f32[1024,1024]{1,0:T(8,128)} fusion(bf16[2048,1024]{0,1:T(8,128)(2,1)} %bitcast.21, bf16[8192,1024]{1,0:T(8,128)(2,1)} %param.4), kind=kOutput, calls=%fused_computation.32 | convolution fusion | flops 4294967296 | bytes 12582912 | tf_op jit(solution)/shard_map/dot_general | solution.py:62
  402.6 8.5 %convolution_convert_fusion.2 = bf16[2048,1024]{1,0:T(8,128)(2,1)} fusion(bf16[2048,1024]{0,1:T(8,128)(2,1)} %bitcast.21, bf16[1024,1024]{1,0:T(8,128)(2,1)S(1)} %bitcast.129), kind=kOutput, calls=%fused_computation.17 | convolution fusion | flops 4297064448 | bytes 10485760 | tf_op jit(solution)/shard_map/dot_general | solution.py:60
  411.0 8.5 %convolution_convert_fusion.4 = bf16[2048,1024]{1,0:T(8,128)(2,1)} fusion(bf16[2048,1024]{0,1:T(8,128)(2,1)} %bitcast.15, bf16[1024,1024]{1,0:T(8,128)(2,1)S(1)} %bitcast.130), kind=kOutput, calls=%fused_computation.19 | convolution fusion | flops 4297064448 | bytes 10485760 | tf_op jit(solution)/shard_map/dot_general | solution.py:60
  419.6 8.3 %fusion.19 = f32[1024,1024]{1,0:T(8,128)} fusion(bf16[2048,1024]{0,1:T(8,128)(2,1)} %bitcast.15, bf16[8192,1024]{1,0:T(8,128)(2,1)S(1)} %bitcast.142), kind=kOutput, calls=%fused_computation.38 | convolution fusion | flops 4294967296 | bytes 12582912 | tf_op jit(solution)/shard_map/dot_general | solution.py:62
  427.9 8.2 %fusion.7 = f32[1024,1024]{1,0:T(8,128)} fusion(bf16[2048,1024]{0,1:T(8,128)(2,1)} %bitcast.27, bf16[8192,1024]{1,0:T(8,128)(2,1)S(1)} %bitcast.142), kind=kOutput, calls=%fused_computation.26 | convolution fusion | flops 4294967296 | bytes 12582912 | tf_op jit(solution)/shard_map/dot_general | solution.py:62
  436.1 14.4 %all-to-all-done.1 = bf16[2048,4,256]{0,2,1:T(8,128)(2,1)} async-done(((bf16[2048,4,256]{0,2,1:T(8,128)(2,1)}), bf16[2048,4,256]{0,2,1:T(8,128)(2,1)}, u32[]{:S(2)}, u32[]{:S(2)}) %all-to-all-start.1) | async-done | bytes 4194336 | tf_op jit(solution)/shard_map/all_to_all | solution.py:57
  450.5 8.7 %convolution_convert_fusion.6 = bf16[2048,1024]{1,0:T(8,128)(2,1)} fusion(bf16[2048,1024]{0,1:T(8,128)(2,1)} %bitcast.7, bf16[1024,1024]{1,0:T(8,128)(2,1)S(1)} %bitcast.131), kind=kOutput, calls=%fused_computation.21 | convolution fusion | flops 4297064448 | bytes 10485760 | tf_op jit(solution)/shard_map/dot_general | solution.py:60
  459.3 10.0 %add_bitcast_fusion = f32[1024,1024]{0,1:T(8,128)} fusion(f32[1024,1024]{1,0:T(8,128)S(1)} %copy-done.16, f32[1024,1024]{1,0:T(8,128)S(1)} %copy-done.14, f32[1024,1024]{1,0:T(8,128)S(1)} %copy-done.15, bf16[2048,1024]{0,1:T(8,128)(2,1)} %bitcast.7, bf16[8192,1024]{1,0:T(8,128)(2,1)} %param.4), kind=kOutput, calls=%fused_computation.14 | convolution fusion | flops 4298113024 | bytes 25165824 | tf_op jit(solution)/shard_map/dot_general | solution.py:62
  469.2 5.6 reshape.153
  484.0 7.6 %convolution_convert_fusion = bf16[2048,1024]{1,0:T(8,128)(2,1)S(1)} fusion(bf16[2048,1024]{0,1:T(8,128)(2,1)} %bitcast.27, bf16[1024,1024]{1,0:T(8,128)(2,1)} %bitcast.128), kind=kOutput, calls=%fused_computation.15 | convolution fusion | flops 4297064448 | bytes 10485760 | tf_op jit(solution)/shard_map/dot_general | solution.py:60
  491.6 8.5 %pad_maximum_fusion = bf16[8192,1024]{1,0:T(8,128)(2,1)} fusion(bf16[2048,1024]{1,0:T(8,128)(2,1)S(1)} %convolution_convert_fusion, bf16[2048,1024]{1,0:T(8,128)(2,1)S(1)} %copy-done.3, bf16[2048,1024]{1,0:T(8,128)(2,1)S(1)} %copy-done.4, bf16[2048,1024]{1,0:T(8,128)(2,1)S(1)} %copy-done.5), kind=kLoop, calls=%fused_computation.2 | loop fusion | flops 67108864 | bytes 33554432 | tf_op jit(solution)/shard_map/concatenate | solution.py:67
  500.2 72.2 %all-reduce.5.cloned.1.call-done = (f32[4,256,256]{2,0,1:T(4,128)}, f32[4,256,256]{2,0,1:T(4,128)}) async-done(((f32[4,256,256]{2,0,1:T(4,128)}, f32[4,256,256]{2,0,1:T(4,128)}), (f32[4,256,256]{2,0,1:T(4,128)}, f32[4,256,256]{2,0,1:T(4,128)})) %all-reduce.5.cloned.1.call-update) | async-done | bytes 2097168
  (86 shorter events, 99.9 us)
Async XLA Ops:
  12.5 9.1 %copy-start.11 = (bf16[128,8,4,256]{3,1,2,0:T(8,128)(2,1)}, bf16[128,8,4,256]{3,1,2,0:T(8,128)(2,1)S(1)}, u32[]{:S(2)}) copy-start(bf16[128,8,4,256]{3,1,2,0:T(8,128)(2,1)S(1)} %copy.43) | copy-start | bytes 6291460
  21.6 53.7 %all-to-all-start.4 = ((bf16[2048,4,256]{0,2,1:T(8,128)(2,1)}), bf16[2048,4,256]{0,2,1:T(8,128)(2,1)}, u32[]{:S(2)}, u32[]{:S(2)}) async-start(bf16[2048,4,256]{0,2,1:T(8,128)(2,1)} %bitcast.125), calls=%async_computation.4 | async-start | bytes 8388608 | tf_op jit(solution)/shard_map/all_to_all | solution.py:48
  75.3 53.5 %all-to-all-start.2 = ((bf16[2048,4,256]{0,2,1:T(8,128)(2,1)}), bf16[2048,4,256]{0,2,1:T(8,128)(2,1)}, u32[]{:S(2)}, u32[]{:S(2)}) async-start(bf16[2048,4,256]{0,2,1:T(8,128)(2,1)} %bitcast.124), calls=%async_computation.2 | async-start | bytes 8388608 | tf_op jit(solution)/shard_map/all_to_all | solution.py:48
  128.9 53.1 %all-to-all-start = ((bf16[2048,4,256]{0,2,1:T(8,128)(2,1)}), bf16[2048,4,256]{0,2,1:T(8,128)(2,1)}, u32[]{:S(2)}, u32[]{:S(2)}) async-start(bf16[2048,4,256]{0,2,1:T(8,128)(2,1)} %bitcast.114), calls=%async_computation | async-start | bytes 8388608 | tf_op jit(solution)/shard_map/all_to_all | solution.py:48
  135.7 3.0 copy-start.13
  135.7 4.3 copy-start.12
  182.0 53.3 %all-to-all-start.6 = ((bf16[2048,4,256]{0,2,1:T(8,128)(2,1)}), bf16[2048,4,256]{0,2,1:T(8,128)(2,1)}, u32[]{:S(2)}, u32[]{:S(2)}) async-start(bf16[2048,4,256]{0,2,1:T(8,128)(2,1)} %bitcast.121), calls=%async_computation.6 | async-start | bytes 8388608 | tf_op jit(solution)/shard_map/all_to_all | solution.py:48
  199.2 3.4 copy-start.8
  235.3 53.1 %all-to-all-start.5 = ((bf16[2048,4,256]{0,2,1:T(8,128)(2,1)}), bf16[2048,4,256]{0,2,1:T(8,128)(2,1)}, u32[]{:S(2)}, u32[]{:S(2)}) async-start(bf16[2048,4,256]{0,2,1:T(8,128)(2,1)} %bitcast.122), calls=%async_computation.5 | async-start | bytes 8388608 | tf_op jit(solution)/shard_map/all_to_all | solution.py:57
  244.6 4.7 copy-start.9
  249.3 8.5 %copy-start.1 = (bf16[2048,4,256]{0,2,1:T(8,128)(2,1)S(1)}, bf16[2048,4,256]{0,2,1:T(8,128)(2,1)}, u32[]{:S(2)}) copy-start(bf16[2048,4,256]{0,2,1:T(8,128)(2,1)} %broadcast_maximum_fusion.1) | copy-start | bytes 12582916
  288.3 53.5 %all-to-all-start.3 = ((bf16[2048,4,256]{0,2,1:T(8,128)(2,1)}), bf16[2048,4,256]{0,2,1:T(8,128)(2,1)}, u32[]{:S(2)}, u32[]{:S(2)}) async-start(bf16[2048,4,256]{0,2,1:T(8,128)(2,1)} %bitcast.120), calls=%async_computation.3 | async-start | bytes 8388608 | tf_op jit(solution)/shard_map/all_to_all | solution.py:57
  293.6 4.6 copy-start.6
  293.6 4.6 copy-start.10
  298.2 8.4 %copy-start = (bf16[2048,4,256]{0,2,1:T(8,128)(2,1)S(1)}, bf16[2048,4,256]{0,2,1:T(8,128)(2,1)}, u32[]{:S(2)}) copy-start(bf16[2048,4,256]{0,2,1:T(8,128)(2,1)} %broadcast_maximum_fusion.2) | copy-start | bytes 12582916
  306.6 8.4 %copy-start.2 = (bf16[2048,4,256]{0,2,1:T(8,128)(2,1)S(1)}, bf16[2048,4,256]{0,2,1:T(8,128)(2,1)}, u32[]{:S(2)}) copy-start(bf16[2048,4,256]{0,2,1:T(8,128)(2,1)} %broadcast_maximum_fusion) | copy-start | bytes 12582916
  341.8 55.5 %all-to-all-start.7 = ((bf16[2048,4,256]{0,2,1:T(8,128)(2,1)}), bf16[2048,4,256]{0,2,1:T(8,128)(2,1)}, u32[]{:S(2)}, u32[]{:S(2)}) async-start(bf16[2048,4,256]{0,2,1:T(8,128)(2,1)} %bitcast.116), calls=%async_computation.7 | async-start | bytes 8388608 | tf_op jit(solution)/shard_map/all_to_all | solution.py:57
  397.3 5.2 copy-start.7
  397.3 53.2 %all-to-all-start.1 = ((bf16[2048,4,256]{0,2,1:T(8,128)(2,1)}), bf16[2048,4,256]{0,2,1:T(8,128)(2,1)}, u32[]{:S(2)}, u32[]{:S(2)}) async-start(bf16[2048,4,256]{0,2,1:T(8,128)(2,1)} %bitcast.119), calls=%async_computation.1 | async-start | bytes 8388608 | tf_op jit(solution)/shard_map/all_to_all | solution.py:57
  402.3 170.0 %all-reduce.5.cloned.1.call-start = ((), (), s32[]{:S(2)}) async-start(), calls=%async_computation.8 | async-start | bytes 4194304
  402.5 17.0 %slice-start = ((s8[16777216]{0:T(1024)(128)(4,1)}), s8[4194304]{0:T(1024)(128)(4,1)S(1)}, s32[]{:S(2)}) async-start(s8[16777216]{0:T(1024)(128)(4,1)} %bitcast.141), calls=%async_computation.9 | async-start | bytes 8388608
  402.6 17.0 %slice-start.1 = ((s8[16777216]{0:T(1024)(128)(4,1)}), s8[4194304]{0:T(1024)(128)(4,1)S(1)}, s32[]{:S(2)}) async-start(s8[16777216]{0:T(1024)(128)(4,1)} %bitcast.141), calls=%async_computation.10 | async-start | bytes 8388608
  411.0 8.6 %slice-start.2 = ((s8[16777216]{0:T(1024)(128)(4,1)}), s8[4194304]{0:T(1024)(128)(4,1)S(1)}, s32[]{:S(2)}) async-start(s8[16777216]{0:T(1024)(128)(4,1)} %bitcast.141), calls=%async_computation.11 | async-start | bytes 8388608
  411.0 8.6 %slice-start.3 = ((s8[16777216]{0:T(1024)(128)(4,1)}), s8[4194304]{0:T(1024)(128)(4,1)S(1)}, s32[]{:S(2)}) async-start(s8[16777216]{0:T(1024)(128)(4,1)} %bitcast.141), calls=%async_computation.12 | async-start | bytes 8388608
  450.5 8.7 %copy-start.14 = (f32[1024,1024]{1,0:T(8,128)S(1)}, f32[1024,1024]{1,0:T(8,128)}, u32[]{:S(2)}) copy-start(f32[1024,1024]{1,0:T(8,128)} %fusion.13) | copy-start | bytes 12582916
  450.5 8.7 %copy-start.15 = (f32[1024,1024]{1,0:T(8,128)S(1)}, f32[1024,1024]{1,0:T(8,128)}, u32[]{:S(2)}) copy-start(f32[1024,1024]{1,0:T(8,128)} %fusion.19) | copy-start | bytes 12582916
  450.5 8.7 %copy-start.16 = (f32[1024,1024]{1,0:T(8,128)S(1)}, f32[1024,1024]{1,0:T(8,128)}, u32[]{:S(2)}) copy-start(f32[1024,1024]{1,0:T(8,128)} %fusion.7) | copy-start | bytes 12582916
  484.0 7.6 %copy-start.3 = (bf16[2048,1024]{1,0:T(8,128)(2,1)S(1)}, bf16[2048,1024]{1,0:T(8,128)(2,1)}, u32[]{:S(2)}) copy-start(bf16[2048,1024]{1,0:T(8,128)(2,1)} %convolution_convert_fusion.2) | copy-start | bytes 12582916
  484.0 7.6 %copy-start.4 = (bf16[2048,1024]{1,0:T(8,128)(2,1)S(1)}, bf16[2048,1024]{1,0:T(8,128)(2,1)}, u32[]{:S(2)}) copy-start(bf16[2048,1024]{1,0:T(8,128)(2,1)} %convolution_convert_fusion.4) | copy-start | bytes 12582916
  484.0 7.6 %copy-start.5 = (bf16[2048,1024]{1,0:T(8,128)(2,1)S(1)}, bf16[2048,1024]{1,0:T(8,128)(2,1)}, u32[]{:S(2)}) copy-start(bf16[2048,1024]{1,0:T(8,128)(2,1)} %convolution_convert_fusion.6) | copy-start | bytes 12582916
Sparse Core Ops, SparseCore 0:
  484.1 88.1 all-reduce.4
where the time goes:
time: 590 us; the launch traced here: 582 us
  waiting for transfers between devices  264 us (45%)
  matrix products  178 us (30%)
  other arithmetic  43.8 us (7%)
  local copies, waits for them, and re-layouts  40.9 us (7%)
  starting transfers between devices  40.3 us (7%)
  between operations  15.3 us (3%)
    all_to_all x4, waiting for transfers between devices, shards(): lax.all_to_all(hidden.reshape(step, n_dev, feat // n_dev), 'tensor', 1, 1...  136 us
    unnamed x2, waiting for transfers between devices  72.2 us
    all_to_all x4, waiting for transfers between devices, shards(): lax.all_to_all(masked.reshape(step, n_dev, feat // n_dev), 'tensor', 1, 1...  55.3 us
    dot_general x4, matrix products, shards(): lax.dot_general(active, cot, (((0,), (0,)), ((), ())), preferred_element_...  38.4 us
    dot_general x4, matrix products, shards(): lax.dot_general(x, returned, (((0,), (0,)), ((), ())), preferred_element_...  36.4 us
    dot_general x4, matrix products, shards(): jnp.dot(x, w1p, preferred_element_type=jnp.float32).astype(jnp.bfloat16)  36.1 us
    dot_general x4, matrix products, shards(): backed = jnp.dot(cot, w2p, preferred_element_type=jnp.float32)  33.5 us
    dot_general x4, matrix products, shards(): jnp.dot(returned, w1tp, preferred_element_type=jnp.float32)  33.3 us
  transfers between devices with their start and end apart: 9, of which 8 were waited for; matrix products, arithmetic and copies ran while one was open for 36% of the time, Pallas kernels for 0%

commit v1 on v0

--- a/solution.py
+++ b/solution.py
@@ -1,3 +1,4 @@
+import functools
 import math
 import jax
 import jax.numpy as jnp
@@ -6,6 +7,34 @@
 
 NB = 16
 CHUNKS = 4
+
+
+def draft_meshes_all(q_in, mesh_ax, d0, array_dim):
+    reached, passed = (lax.axis_size(mesh_ax), lax.axis_index(mesh_ax))
+    parts_out = q_in.shape[d0] // reached
+    q_next = list(q_in.shape)
+    q_next[d0] = parts_out
+    newest = q_next[array_dim]
+    q_next[array_dim] = newest * reached
+    prior = jnp.zeros(q_next, q_in.dtype)
+    rr = 0
+    while rr < reached:
+        value_now = lax.dynamic_slice_in_dim(q_in, (passed ^ rr) * parts_out, parts_out, axis=d0)
+        if rr:
+            line_up = []
+            it = 0
+            while it < reached:
+                line_up.append((it, it ^ rr))
+                it = it + 1
+            value_now = lax.ppermute(value_now, axis_name=mesh_ax, perm=line_up)
+        prior = lax.dynamic_update_slice_in_dim(
+            prior, value_now, (passed ^ rr) * newest, axis=array_dim
+        )
+        rr += 1
+    return prior
+
+
+track_node = functools.partial(draft_meshes_all, mesh_ax="tensor", d0=1, array_dim=1)
 
 
 def expanded_weights(w_first, w_second, n_dev):
@@ -45,9 +74,7 @@
         x = tokens[k * step : (k + 1) * step]
         cot = cotangent[k * step : (k + 1) * step]
         hidden = jnp.dot(x, w1p, preferred_element_type=jnp.float32).astype(jnp.bfloat16)
-        moved = lax.all_to_all(
-            hidden.reshape(step, n_dev, feat // n_dev), "tensor", 1, 1, tiled=True
-        ).reshape(step, feat)
+        moved = track_node(hidden.reshape(step, n_dev, feat // n_dev)).reshape(step, feat)
         active = jnp.maximum(moved, jnp.zeros((), jnp.bfloat16))
         gs = lax.dot_general(
             active, cot, (((0,), (0,)), ((), ())), preferred_element_type=jnp.float32

time: 590 us -> 569 us (0.964)
  local copies, waits for them, and re-layouts: 40.9 us -> 77.3 us
  waiting for transfers between devices: 264 us -> 243 us
  matrix products: 178 us -> 161 us
  starting transfers between devices: 40.3 us -> 28.3 us
  other arithmetic: 43.8 us -> 36.2 us
    all_to_all x4 -> x0, waiting for transfers between devices: 136 us -> none  [shards(): lax.all_to_all(hidden.reshape(step, n_dev, feat // n_dev), 'tensor', 1, 1...]
    ppermute x0 -> x12, waiting for transfers between devices: none -> 111 us  [draft_meshes_all(): value_now = lax.ppermute(value_now, axis_name=mesh_ax, perm=line_up)]
    all_to_all x4 -> x0, starting transfers between devices: 20.1 us -> none  [shards(): lax.all_to_all(hidden.reshape(step, n_dev, feat // n_dev), 'tensor', 1, 1...]
    dynamic_update_slice x0 -> x12, local copies, waits for them, and re-layouts: none -> 16.4 us  [draft_meshes_all(): lax.dynamic_update_slice_in_dim(prior, value_now, (passed ^ rr) * newest,...]
    dot_general x4, matrix products: 36.1 us -> 23.4 us  [shards(): jnp.dot(x, w1p, preferred_element_type=jnp.float32).astype(jnp.bfloat16)]
    ppermute x0 -> x12, starting transfers between devices: none -> 8.52 us  [draft_meshes_all(): value_now = lax.ppermute(value_now, axis_name=mesh_ax, perm=line_up)]
    another operation x0 -> x4, local copies, waits for them, and re-layouts: none -> 8.18 us
    dynamic_slice x0 -> x4, local copies, waits for them, and re-layouts: none -> 7.06 us  [draft_meshes_all(): lax.dynamic_slice_in_dim(q_in, (passed ^ rr) * parts_out, parts_out, axis...]
  transfers between devices with their start and end apart: 9 -> 17, of which waited for: 8 -> 9; matrix products, arithmetic and copies ran while one was open for 36% -> 39% of each run, Pallas kernels for 0% -> 0%
where the time goes in v1:
time: 569 us; the launch traced here: 562 us
  waiting for transfers between devices  243 us (43%)
  matrix products  161 us (28%)
  local copies, waits for them, and re-layouts  77.3 us (14%)
  other arithmetic  36.2 us (6%)
  starting transfers between devices  28.3 us (5%)
  between operations  15.7 us (3%)
    ppermute x12, waiting for transfers between devices, draft_meshes_all(): value_now = lax.ppermute(value_now, axis_name=mesh_ax, perm=line_up)  111 us
    unnamed x2, waiting for transfers between devices  71.4 us
    all_to_all x4, waiting for transfers between devices, shards(): lax.all_to_all(masked.reshape(step, n_dev, feat // n_dev), 'tensor', 1, 1...  60.6 us
    dot_general x4, matrix products, shards(): lax.dot_general(x, returned, (((0,), (0,)), ((), ())), preferred_element_...  36.6 us
    dot_general x4, matrix products, shards(): backed = jnp.dot(cot, w2p, preferred_element_type=jnp.float32)  34 us
    dot_general x4, matrix products, shards(): lax.dot_general(active, cot, (((0,), (0,)), ((), ())), preferred_element_...  33.8 us
    dot_general x4, matrix products, shards(): jnp.dot(returned, w1tp, preferred_element_type=jnp.float32)  33.6 us
    dot_general x4, matrix products, shards(): jnp.dot(x, w1p, preferred_element_type=jnp.float32).astype(jnp.bfloat16)  23.4 us
  transfers between devices with their start and end apart: 17, of which 9 were waited for; matrix products, arithmetic and copies ran while one was open for 39% of the time, Pallas kernels for 0%

profile of v1, /device:TPU:0, one launch (start us, length us, event | category | flops | bytes accessed | tf_op | source)
XLA Modules:
  0.0 561.9 jit_solution(7357868802011594235)
XLA Ops:
  13.8 7.5 %convolution_convert_fusion.5 = bf16[1024,2048]{1,0:T(8,128)(2,1)S(1)} fusion(bf16[1024,1024]{0,1:T(8,128)(2,1)} %bitcast.136, bf16[8192,1024]{1,0:T(8,128)(2,1)} %param.4), kind=kOutput, calls=%fused_computation.20 | convolution fusion | flops 4297064448 | bytes 10485760 | tf_op jit(solution)/shard_map/dot_general | solution.py:76
  45.7 6.1 %convolution_convert_fusion.1 = bf16[1024,2048]{1,0:T(8,128)(2,1)} fusion(bf16[1024,1024]{0,1:T(8,128)(2,1)S(1)} %bitcast.139, bf16[8192,1024]{1,0:T(8,128)(2,1)S(1)} %bitcast.144), kind=kOutput, calls=%fused_computation.16 | convolution fusion | flops 4297064448 | bytes 10485760 | tf_op jit(solution)/shard_map/dot_general | solution.py:76
  82.8 8.8 %fusion.2 = bf16[2048,1024]{0,1:T(8,128)(2,1)} fusion(pred[2048,4,256]{0,2,1:T(32,128)(4,1)S(1)} %broadcast_compare_fusion.2, bf16[1024,1024]{0,1:T(8,128)(2,1)S(1)} %bitcast.132, bf16[8192,1024]{1,0:T(8,128)(2,1)} %param.5), kind=kOutput, calls=%fused_computation.8 | convolution fusion | flops 4299161600 | bytes 12582912 | tf_op jit(solution)/shard_map/dot_general | solution.py:82
  92.9 50.3 %collective-permute-done.7 = bf16[2048,1,256]{0,2,1:T(8,128)(2,1)S(1)} collective-permute-done((bf16[2048,1,256]{0,2,1:T(8,128)(2,1)S(1)}, bf16[2048,1,256]{0,2,1:T(8,128)(2,1)S(1)}, u32[]{:S(2)}, u32[]{:S(2)}) %collective-permute-start.7) | collective-permute-done | bytes 1048608 | tf_op jit(solution)/shard_map/ppermute | solution.py:29
  148.9 16.5 %collective-permute-done.8 = bf16[2048,1,256]{0,2,1:T(8,128)(2,1)S(1)} collective-permute-done((bf16[2048,1,256]{0,2,1:T(8,128)(2,1)S(1)}, bf16[2048,1,256]{0,2,1:T(8,128)(2,1)S(1)}, u32[]{:S(2)}, u32[]{:S(2)}) %collective-permute-start.8) | collective-permute-done | bytes 1048608 | tf_op jit(solution)/shard_map/ppermute | solution.py:29
  172.5 18.9 %collective-permute-done.10 = bf16[2048,1,256]{0,2,1:T(8,128)(2,1)S(1)} collective-permute-done((bf16[2048,1,256]{0,2,1:T(8,128)(2,1)S(1)}, bf16[2048,1,256]{0,2,1:T(8,128)(2,1)S(1)}, u32[]{:S(2)}, u32[]{:S(2)}) %collective-permute-start.10) | collective-permute-done | bytes 1048608 | tf_op jit(solution)/shard_map/ppermute | solution.py:29
  191.5 20.7 %collective-permute-done.11 = bf16[2048,1,256]{0,2,1:T(8,128)(2,1)S(1)} collective-permute-done((bf16[2048,1,256]{0,2,1:T(8,128)(2,1)S(1)}, bf16[2048,1,256]{0,2,1:T(8,128)(2,1)S(1)}, u32[]{:S(2)}, u32[]{:S(2)}) %collective-permute-start.11) | collective-permute-done | bytes 1048608 | tf_op jit(solution)/shard_map/ppermute | solution.py:29
  230.7 8.4 %fusion.1 = bf16[2048,1024]{0,1:T(8,128)(2,1)} fusion(pred[2048,4,256]{0,2,1:T(32,128)(4,1)S(1)} %broadcast_compare_fusion.1, bf16[1024,1024]{0,1:T(8,128)(2,1)S(1)} %bitcast.133, bf16[8192,1024]{1,0:T(8,128)(2,1)} %param.5), kind=kOutput, calls=%fused_computation.6 | convolution fusion | flops 4299161600 | bytes 12582912 | tf_op jit(solution)/shard_map/dot_general | solution.py:82
  239.1 8.2 %fusion.16 = f32[1024,1024]{1,0:T(8,128)} fusion(bf16[2048,1024]{0,1:T(8,128)(2,1)S(1)} %bitcast.119, bf16[8192,1024]{1,0:T(8,128)(2,1)} %param.5), kind=kOutput, calls=%fused_computation.35 | convolution fusion | flops 4294967296 | bytes 12582912 | tf_op jit(solution)/shard_map/dot_general | solution.py:79
  247.3 21.5 %all-to-all-done.1 = bf16[2048,4,256]{0,2,1:T(8,128)(2,1)} async-done(((bf16[2048,4,256]{0,2,1:T(8,128)(2,1)}), bf16[2048,4,256]{0,2,1:T(8,128)(2,1)}, u32[]{:S(2)}, u32[]{:S(2)}) %all-to-all-start.1) | async-done | bytes 4194336 | tf_op jit(solution)/shard_map/all_to_all | solution.py:84
  276.6 8.5 %fusion = bf16[2048,1024]{0,1:T(8,128)(2,1)} fusion(pred[2048,4,256]{0,2,1:T(32,128)(4,1)S(1)} %broadcast_compare_fusion, bf16[1024,1024]{0,1:T(8,128)(2,1)S(1)} %bitcast.134, bf16[8192,1024]{1,0:T(8,128)(2,1)} %param.5), kind=kOutput, calls=%fused_computation.4 | convolution fusion | flops 4299161600 | bytes 12582912 | tf_op jit(solution)/shard_map/dot_general | solution.py:82
  285.1 6.1 %fusion.22 = f32[1024,1024]{1,0:T(8,128)} fusion(bf16[2048,1024]{0,1:T(8,128)(2,1)S(1)} %bitcast.125, bf16[8192,1024]{1,0:T(8,128)(2,1)S(1)} %bitcast.142), kind=kOutput, calls=%fused_computation.41 | convolution fusion | flops 4294967296 | bytes 12582912 | tf_op jit(solution)/shard_map/dot_general | solution.py:79
  291.2 6.0 %fusion.10 = f32[1024,1024]{1,0:T(8,128)} fusion(bf16[2048,1024]{0,1:T(8,128)(2,1)S(1)} %bitcast.120, bf16[8192,1024]{1,0:T(8,128)(2,1)S(1)} %bitcast.142), kind=kOutput, calls=%fused_computation.29 | convolution fusion | flops 4294967296 | bytes 12582912 | tf_op jit(solution)/shard_map/dot_general | solution.py:79
  297.2 24.7 %all-to-all-done.2 = bf16[2048,4,256]{0,2,1:T(8,128)(2,1)} async-done(((bf16[2048,4,256]{0,2,1:T(8,128)(2,1)}), bf16[2048,4,256]{0,2,1:T(8,128)(2,1)}, u32[]{:S(2)}, u32[]{:S(2)}) %all-to-all-start.2) | async-done | bytes 4194336 | tf_op jit(solution)/shard_map/all_to_all | solution.py:84
  321.9 5.0 all-to-all-start.3
  327.0 13.5 %add_add_fusion = f32[1024,1024]{1,0:T(8,128)} fusion(f32[1024,1024]{1,0:T(8,128)} %fusion.10, f32[1024,1024]{1,0:T(8,128)} %fusion.22, f32[1024,1024]{1,0:T(8,128)} %fusion.16, bf16[2048,1024]{0,1:T(8,128)(2,1)} %bitcast.121, bf16[8192,1024]{1,0:T(8,128)(2,1)} %param.5), kind=kOutput, calls=%fused_computation.13 | convolution fusion | flops 4298113024 | bytes 25165824 | tf_op jit(solution)/shard_map/dot_general | solution.py:79
  340.5 5.6 reshape.154
  346.1 5.2 copy.48
  359.2 8.3 %fusion.3 = bf16[2048,1024]{0,1:T(8,128)(2,1)} fusion(pred[2048,4,256]{0,2,1:T(32,128)(4,1)S(1)} %broadcast_compare_fusion.3, bf16[1024,1024]{0,1:T(8,128)(2,1)S(1)} %bitcast.135, bf16[8192,1024]{1,0:T(8,128)(2,1)} %param.5), kind=kOutput, calls=%fused_computation.10 | convolution fusion | flops 4299161600 | bytes 12582912 | tf_op jit(solution)/shard_map/dot_general | solution.py:82
  367.5 10.0 %fusion.19 = f32[1024,1024]{1,0:T(8,128)} fusion(bf16[2048,1024]{0,1:T(8,128)(2,1)} %bitcast.17, bf16[8192,1024]{1,0:T(8,128)(2,1)} %param.4), kind=kOutput, calls=%fused_computation.38 | convolution fusion | flops 4294967296 | bytes 12582912 | tf_op jit(solution)/shard_map/dot_general | solution.py:89
  377.5 5.0 all-to-all-start
  382.6 8.8 %convolution_convert_fusion.4 = bf16[2048,1024]{1,0:T(8,128)(2,1)} fusion(bf16[2048,1024]{0,1:T(8,128)(2,1)} %bitcast.17, bf16[1024,1024]{1,0:T(8,128)(2,1)S(1)} %bitcast.129), kind=kOutput, calls=%fused_computation.19 | convolution fusion | flops 4297064448 | bytes 10485760 | tf_op jit(solution)/shard_map/dot_general | solution.py:87
  391.4 8.4 %convolution_convert_fusion.2 = bf16[2048,1024]{1,0:T(8,128)(2,1)} fusion(bf16[2048,1024]{0,1:T(8,128)(2,1)} %bitcast.24, bf16[1024,1024]{1,0:T(8,128)(2,1)S(1)} %bitcast.130), kind=kOutput, calls=%fused_computation.17 | convolution fusion | flops 4297064448 | bytes 10485760 | tf_op jit(solution)/shard_map/dot_general | solution.py:87
  399.9 8.3 %fusion.13 = f32[1024,1024]{1,0:T(8,128)} fusion(bf16[2048,1024]{0,1:T(8,128)(2,1)} %bitcast.24, bf16[8192,1024]{1,0:T(8,128)(2,1)S(1)} %bitcast.146), kind=kOutput, calls=%fused_computation.32 | convolution fusion | flops 4294967296 | bytes 12582912 | tf_op jit(solution)/shard_map/dot_general | solution.py:89
  408.2 8.3 %fusion.7 = f32[1024,1024]{1,0:T(8,128)} fusion(bf16[2048,1024]{0,1:T(8,128)(2,1)} %bitcast.31, bf16[8192,1024]{1,0:T(8,128)(2,1)S(1)} %bitcast.146), kind=kOutput, calls=%fused_computation.26 | convolution fusion | flops 4294967296 | bytes 12582912 | tf_op jit(solution)/shard_map/dot_general | solution.py:89
  416.4 14.3 %all-to-all-done = bf16[2048,4,256]{0,2,1:T(8,128)(2,1)} async-done(((bf16[2048,4,256]{0,2,1:T(8,128)(2,1)}), bf16[2048,4,256]{0,2,1:T(8,128)(2,1)}, u32[]{:S(2)}, u32[]{:S(2)}) %all-to-all-start) | async-done | bytes 4194336 | tf_op jit(solution)/shard_map/all_to_all | solution.py:84
  430.8 8.8 %convolution_convert_fusion.6 = bf16[2048,1024]{1,0:T(8,128)(2,1)} fusion(bf16[2048,1024]{0,1:T(8,128)(2,1)} %bitcast.8, bf16[1024,1024]{1,0:T(8,128)(2,1)S(1)} %bitcast.131), kind=kOutput, calls=%fused_computation.21 | convolution fusion | flops 4297064448 | bytes 10485760 | tf_op jit(solution)/shard_map/dot_general | solution.py:87
  439.6 10.1 %add_bitcast_fusion = f32[1024,1024]{0,1:T(8,128)} fusion(f32[1024,1024]{1,0:T(8,128)S(1)} %copy-done.21, f32[1024,1024]{1,0:T(8,128)S(1)} %copy-done.20, f32[1024,1024]{1,0:T(8,128)S(1)} %copy-done.19, bf16[2048,1024]{0,1:T(8,128)(2,1)} %bitcast.8, bf16[8192,1024]{1,0:T(8,128)(2,1)} %param.4), kind=kOutput, calls=%fused_computation.14 | convolution fusion | flops 4298113024 | bytes 25165824 | tf_op jit(solution)/shard_map/dot_general | solution.py:89
  449.7 5.6 reshape.153
  464.5 7.6 %convolution_convert_fusion = bf16[2048,1024]{1,0:T(8,128)(2,1)S(1)} fusion(bf16[2048,1024]{0,1:T(8,128)(2,1)} %bitcast.31, bf16[1024,1024]{1,0:T(8,128)(2,1)} %bitcast.128), kind=kOutput, calls=%fused_computation.15 | convolution fusion | flops 4297064448 | bytes 10485760 | tf_op jit(solution)/shard_map/dot_general | solution.py:87
  472.1 8.5 %pad_maximum_fusion = bf16[8192,1024]{1,0:T(8,128)(2,1)} fusion(bf16[2048,1024]{1,0:T(8,128)(2,1)S(1)} %convolution_convert_fusion, bf16[2048,1024]{1,0:T(8,128)(2,1)S(1)} %copy-done.6, bf16[2048,1024]{1,0:T(8,128)(2,1)S(1)} %copy-done.5, bf16[2048,1024]{1,0:T(8,128)(2,1)S(1)} %copy-done.7), kind=kLoop, calls=%fused_computation.2 | loop fusion | flops 67108864 | bytes 33554432 | tf_op jit(solution)/shard_map/concatenate | solution.py:94
  480.7 71.4 %all-reduce.5.cloned.1.call-done = (f32[4,256,256]{2,0,1:T(4,128)}, f32[4,256,256]{2,0,1:T(4,128)}) async-done(((f32[4,256,256]{2,0,1:T(4,128)}, f32[4,256,256]{2,0,1:T(4,128)}), (f32[4,256,256]{2,0,1:T(4,128)}, f32[4,256,256]{2,0,1:T(4,128)})) %all-reduce.5.cloned.1.call-update) | async-done | bytes 2097168
  (150 shorter events, 121.3 us)
Async XLA Ops:
  13.8 15.5 %slice-start.4 = ((s8[16777216]{0:T(1024)(128)(4,1)}), s8[4194304]{0:T(1024)(128)(4,1)S(1)}, s32[]{:S(2)}) async-start(s8[16777216]{0:T(1024)(128)(4,1)} %bitcast.143), calls=%async_computation.9 | async-start | bytes 8388608
  13.8 15.5 %slice-start.5 = ((s8[16777216]{0:T(1024)(128)(4,1)}), s8[4194304]{0:T(1024)(128)(4,1)S(1)}, s32[]{:S(2)}) async-start(s8[16777216]{0:T(1024)(128)(4,1)} %bitcast.143), calls=%async_computation.10 | async-start | bytes 8388608
  13.8 15.5 %slice-start.6 = ((s8[16777216]{0:T(1024)(128)(4,1)}), s8[4194304]{0:T(1024)(128)(4,1)S(1)}, s32[]{:S(2)}) async-start(s8[16777216]{0:T(1024)(128)(4,1)} %bitcast.143), calls=%async_computation.11 | async-start | bytes 8388608
  26.2 39.3 %collective-permute-start.3 = (bf16[2048,1,256]{0,2,1:T(8,128)(2,1)}, bf16[2048,1,256]{0,2,1:T(8,128)(2,1)}, u32[]{:S(2)}, u32[]{:S(2)}) collective-permute-start(bf16[2048,1,256]{0,2,1:T(8,128)(2,1)} %get-tuple-element.20), channel_id=1, source_target_pairs={{0,4},{4,0},{8,12},{12,8},{1,5},{5,1},{9,13},{13,9},{2,6},{6,2},{1... | collective-permute-start | bytes 3145736 | tf_op jit(solution)/shard_map/ppermute | solution.py:29
  26.7 41.8 %collective-permute-start.4 = (bf16[2048,1,256]{0,2,1:T(8,128)(2,1)}, bf16[2048,1,256]{0,2,1:T(8,128)(2,1)}, u32[]{:S(2)}, u32[]{:S(2)}) collective-permute-start(bf16[2048,1,256]{0,2,1:T(8,128)(2,1)} %get-tuple-element.19), channel_id=1, source_target_pairs={{0,8},{4,12},{8,0},{12,4},{1,9},{5,13},{9,1},{13,5},{2,10},{6,14},... | collective-permute-start | bytes 3145736 | tf_op jit(solution)/shard_map/ppermute | solution.py:29
  29.1 46.4 %collective-permute-start.5 = (bf16[2048,1,256]{0,2,1:T(8,128)(2,1)}, bf16[2048,1,256]{0,2,1:T(8,128)(2,1)}, u32[]{:S(2)}, u32[]{:S(2)}) collective-permute-start(bf16[2048,1,256]{0,2,1:T(8,128)(2,1)} %get-tuple-element.18), channel_id=1, source_target_pairs={{0,12},{4,8},{8,4},{12,0},{1,13},{5,9},{9,5},{13,1},{2,14},{6,10},... | collective-permute-start | bytes 3145736 | tf_op jit(solution)/shard_map/ppermute | solution.py:29
  38.9 181.5 %collective-permute-start = (bf16[2048,1,256]{0,2,1:T(8,128)(2,1)}, bf16[2048,1,256]{0,2,1:T(8,128)(2,1)}, u32[]{:S(2)}, u32[]{:S(2)}) collective-permute-start(bf16[2048,1,256]{0,2,1:T(8,128)(2,1)} %get-tuple-element.16), channel_id=1, source_target_pairs={{0,4},{4,0},{8,12},{12,8},{1,5},{5,1},{9,13},{13,9},{2,6},{6,2},{1... | collective-permute-start | bytes 3145736 | tf_op jit(solution)/shard_map/ppermute | solution.py:29
  39.0 187.1 %collective-permute-start.1 = (bf16[2048,1,256]{0,2,1:T(8,128)(2,1)}, bf16[2048,1,256]{0,2,1:T(8,128)(2,1)}, u32[]{:S(2)}, u32[]{:S(2)}) collective-permute-start(bf16[2048,1,256]{0,2,1:T(8,128)(2,1)} %get-tuple-element.15), channel_id=1, source_target_pairs={{0,8},{4,12},{8,0},{12,4},{1,9},{5,13},{9,1},{13,5},{2,10},{6,14},... | collective-permute-start | bytes 3145736 | tf_op jit(solution)/shard_map/ppermute | solution.py:29
  65.5 10.0 %copy-start.16 = (bf16[2048,1,256]{0,2,1:T(8,128)(2,1)S(1)}, bf16[2048,1,256]{0,2,1:T(8,128)(2,1)}, u32[]{:S(2)}) copy-start(bf16[2048,1,256]{0,2,1:T(8,128)(2,1)} %get-tuple-element.23) | copy-start | bytes 3145732
  66.2 162.3 %collective-permute-start.2 = (bf16[2048,1,256]{0,2,1:T(8,128)(2,1)S(1)}, bf16[2048,1,256]{0,2,1:T(8,128)(2,1)S(1)}, u32[]{:S(2)}, u32[]{:S(2)}) collective-permute-start(bf16[2048,1,256]{0,2,1:T(8,128)(2,1)S(1)} %copy-done.14), channel_id=1, source_target_pairs={{0,12},{4,8},{8,4},{12,0},{1,13},{5,9},{9,5},{13,1},{2,14},{6,10},... | collective-permute-start | bytes 3145736 | tf_op jit(solution)/shard_map/ppermute | solution.py:29
  68.5 23.1 %collective-permute-start.6 = (bf16[2048,1,256]{0,2,1:T(8,128)(2,1)S(1)}, bf16[2048,1,256]{0,2,1:T(8,128)(2,1)S(1)}, u32[]{:S(2)}, u32[]{:S(2)}) collective-permute-start(bf16[2048,1,256]{0,2,1:T(8,128)(2,1)S(1)} %copy-done.17), channel_id=1, source_target_pairs={{0,4},{4,0},{8,12},{12,8},{1,5},{5,1},{9,13},{13,9},{2,6},{6,2},{1... | collective-permute-start | bytes 3145736 | tf_op jit(solution)/shard_map/ppermute | solution.py:29
  75.6 67.7 %collective-permute-start.7 = (bf16[2048,1,256]{0,2,1:T(8,128)(2,1)S(1)}, bf16[2048,1,256]{0,2,1:T(8,128)(2,1)S(1)}, u32[]{:S(2)}, u32[]{:S(2)}) collective-permute-start(bf16[2048,1,256]{0,2,1:T(8,128)(2,1)S(1)} %copy-done.16), channel_id=1, source_target_pairs={{0,8},{4,12},{8,0},{12,4},{1,9},{5,13},{9,1},{13,5},{2,10},{6,14},... | collective-permute-start | bytes 3145736 | tf_op jit(solution)/shard_map/ppermute | solution.py:29
  82.8 8.8 %copy-start.15 = (bf16[2048,1,256]{0,2,1:T(8,128)(2,1)S(1)}, bf16[2048,1,256]{0,2,1:T(8,128)(2,1)}, u32[]{:S(2)}) copy-start(bf16[2048,1,256]{0,2,1:T(8,128)(2,1)} %get-tuple-element.22) | copy-start | bytes 3145732
  91.6 73.8 %collective-permute-start.8 = (bf16[2048,1,256]{0,2,1:T(8,128)(2,1)S(1)}, bf16[2048,1,256]{0,2,1:T(8,128)(2,1)S(1)}, u32[]{:S(2)}, u32[]{:S(2)}) collective-permute-start(bf16[2048,1,256]{0,2,1:T(8,128)(2,1)S(1)} %copy-done.15), channel_id=1, source_target_pairs={{0,12},{4,8},{8,4},{12,0},{1,13},{5,9},{9,5},{13,1},{2,14},{6,10},... | collective-permute-start | bytes 3145736 | tf_op jit(solution)/shard_map/ppermute | solution.py:29
  143.2 24.7 %collective-permute-start.9 = (bf16[2048,1,256]{0,2,1:T(8,128)(2,1)S(1)}, bf16[2048,1,256]{0,2,1:T(8,128)(2,1)S(1)}, u32[]{:S(2)}, u32[]{:S(2)}) collective-permute-start(bf16[2048,1,256]{0,2,1:T(8,128)(2,1)S(1)} %get-tuple-element.28), channel_id=1, source_target_pairs={{0,4},{4,0},{8,12},{12,8},{1,5},{5,1},{9,13},{13,9},{2,6},{6,2},{1... | collective-permute-start | bytes 3145736 | tf_op jit(solution)/shard_map/ppermute | solution.py:29
  165.3 26.0 %collective-permute-start.10 = (bf16[2048,1,256]{0,2,1:T(8,128)(2,1)S(1)}, bf16[2048,1,256]{0,2,1:T(8,128)(2,1)S(1)}, u32[]{:S(2)}, u32[]{:S(2)}) collective-permute-start(bf16[2048,1,256]{0,2,1:T(8,128)(2,1)S(1)} %get-tuple-element.27), channel_id=1, source_target_pairs={{0,8},{4,12},{8,0},{12,4},{1,9},{5,13},{9,1},{13,5},{2,10},{6,14},... | collective-permute-start | bytes 3145736 | tf_op jit(solution)/shard_map/ppermute | solution.py:29
  168.0 44.2 %collective-permute-start.11 = (bf16[2048,1,256]{0,2,1:T(8,128)(2,1)S(1)}, bf16[2048,1,256]{0,2,1:T(8,128)(2,1)S(1)}, u32[]{:S(2)}, u32[]{:S(2)}) collective-permute-start(bf16[2048,1,256]{0,2,1:T(8,128)(2,1)S(1)} %get-tuple-element.26), channel_id=1, source_target_pairs={{0,12},{4,8},{8,4},{12,0},{1,13},{5,9},{9,5},{13,1},{2,14},{6,10},... | collective-permute-start | bytes 3145736 | tf_op jit(solution)/shard_map/ppermute | solution.py:29
  215.6 53.3 %all-to-all-start.1 = ((bf16[2048,4,256]{0,2,1:T(8,128)(2,1)}), bf16[2048,4,256]{0,2,1:T(8,128)(2,1)}, u32[]{:S(2)}, u32[]{:S(2)}) async-start(bf16[2048,4,256]{0,2,1:T(8,128)(2,1)} %bitcast.118), calls=%async_computation.1 | async-start | bytes 8388608 | tf_op jit(solution)/shard_map/all_to_all | solution.py:84
  268.8 53.1 %all-to-all-start.2 = ((bf16[2048,4,256]{0,2,1:T(8,128)(2,1)}), bf16[2048,4,256]{0,2,1:T(8,128)(2,1)}, u32[]{:S(2)}, u32[]{:S(2)}) async-start(bf16[2048,4,256]{0,2,1:T(8,128)(2,1)} %bitcast.124), calls=%async_computation.2 | async-start | bytes 8388608 | tf_op jit(solution)/shard_map/all_to_all | solution.py:84
  273.7 11.4 %slice-start = ((s8[16777216]{0:T(1024)(128)(4,1)}), s8[4194304]{0:T(1024)(128)(4,1)S(1)}, s32[]{:S(2)}) async-start(s8[16777216]{0:T(1024)(128)(4,1)} %bitcast.141), calls=%async_computation.5 | async-start | bytes 8388608
  276.6 8.5 %slice-start.1 = ((s8[16777216]{0:T(1024)(128)(4,1)}), s8[4194304]{0:T(1024)(128)(4,1)S(1)}, s32[]{:S(2)}) async-start(s8[16777216]{0:T(1024)(128)(4,1)} %bitcast.141), calls=%async_computation.6 | async-start | bytes 8388608
  276.6 8.5 %slice-start.2 = ((s8[16777216]{0:T(1024)(128)(4,1)}), s8[4194304]{0:T(1024)(128)(4,1)S(1)}, s32[]{:S(2)}) async-start(s8[16777216]{0:T(1024)(128)(4,1)} %bitcast.141), calls=%async_computation.7 | async-start | bytes 8388608
  276.6 8.6 %slice-start.3 = ((s8[16777216]{0:T(1024)(128)(4,1)}), s8[4194304]{0:T(1024)(128)(4,1)S(1)}, s32[]{:S(2)}) async-start(s8[16777216]{0:T(1024)(128)(4,1)} %bitcast.141), calls=%async_computation.8 | async-start | bytes 8388608
  321.9 55.6 %all-to-all-start.3 = ((bf16[2048,4,256]{0,2,1:T(8,128)(2,1)}), bf16[2048,4,256]{0,2,1:T(8,128)(2,1)}, u32[]{:S(2)}, u32[]{:S(2)}) async-start(bf16[2048,4,256]{0,2,1:T(8,128)(2,1)} %bitcast.122), calls=%async_computation.3 | async-start | bytes 8388608 | tf_op jit(solution)/shard_map/all_to_all | solution.py:84
  377.5 53.2 %all-to-all-start = ((bf16[2048,4,256]{0,2,1:T(8,128)(2,1)}), bf16[2048,4,256]{0,2,1:T(8,128)(2,1)}, u32[]{:S(2)}, u32[]{:S(2)}) async-start(bf16[2048,4,256]{0,2,1:T(8,128)(2,1)} %bitcast.123), calls=%async_computation | async-start | bytes 8388608 | tf_op jit(solution)/shard_map/all_to_all | solution.py:84
  382.5 169.5 %all-reduce.5.cloned.1.call-start = ((), (), s32[]{:S(2)}) async-start(), calls=%async_computation.4 | async-start | bytes 4194304
  382.6 17.3 %slice-start.8 = ((s8[16777216]{0:T(1024)(128)(4,1)}), s8[4194304]{0:T(1024)(128)(4,1)S(1)}, s32[]{:S(2)}) async-start(s8[16777216]{0:T(1024)(128)(4,1)} %bitcast.145), calls=%async_computation.13 | async-start | bytes 8388608
  382.6 17.3 %slice-start.9 = ((s8[16777216]{0:T(1024)(128)(4,1)}), s8[4194304]{0:T(1024)(128)(4,1)S(1)}, s32[]{:S(2)}) async-start(s8[16777216]{0:T(1024)(128)(4,1)} %bitcast.145), calls=%async_computation.14 | async-start | bytes 8388608
  391.4 8.5 %slice-start.11 = ((s8[16777216]{0:T(1024)(128)(4,1)}), s8[4194304]{0:T(1024)(128)(4,1)S(1)}, s32[]{:S(2)}) async-start(s8[16777216]{0:T(1024)(128)(4,1)} %bitcast.145), calls=%async_computation.16 | async-start | bytes 8388608
  430.8 8.8 %copy-start.19 = (f32[1024,1024]{1,0:T(8,128)S(1)}, f32[1024,1024]{1,0:T(8,128)}, u32[]{:S(2)}) copy-start(f32[1024,1024]{1,0:T(8,128)} %fusion.19) | copy-start | bytes 12582916
  430.8 8.8 %copy-start.20 = (f32[1024,1024]{1,0:T(8,128)S(1)}, f32[1024,1024]{1,0:T(8,128)}, u32[]{:S(2)}) copy-start(f32[1024,1024]{1,0:T(8,128)} %fusion.13) | copy-start | bytes 12582916
  430.8 8.8 %copy-start.21 = (f32[1024,1024]{1,0:T(8,128)S(1)}, f32[1024,1024]{1,0:T(8,128)}, u32[]{:S(2)}) copy-start(f32[1024,1024]{1,0:T(8,128)} %fusion.7) | copy-start | bytes 12582916
  (19 other events, 102.2 us)
Sparse Core Ops, SparseCore 0:
  464.6 87.4 all-reduce.4
